TPU v7x, 32 devices: a whole 2x2x4 slice. The times are simulated.
32 devices in a mesh: dp: 8 (over z, x), tensor: 4 (over y, core).
Axes of the slice: x: 2, y: 2, z: 4, core: 2. Of those that a mesh axis runs over, the one named last changes fastest.
Arguments:
- tokens: bfloat16 [2048, 4096], P('dp', 'tensor'), may hold values from -6 to 6
- norm_gain: float32 [4096], replicated, may hold values from 0.15 to 5.4, as said below
- w_query: bfloat16 [4096, 4096], P(None, 'tensor'), may hold values from -0.09375 to 0.09375
- key_weight: bfloat16 [4096, 1024], P(None, 'tensor'), may hold values from -0.09375 to 0.09375
- value_weight: bfloat16 [4096, 1024], P(None, 'tensor'), may hold values from -0.09375 to 0.09375
- w_out: bfloat16 [4096, 4096], P('tensor'), may hold values from -0.25 to 0.25
- grad_output: bfloat16 [2048, 4096], P('dp', 'tensor'), may hold values from -6 to 6
- doc_lengths: int32 [8, 2], P('dp'), may hold values from 0 to 256, as said below
- block_owner: int32 [8, 8], replicated, may hold values from 0 to 7, as said below
Outputs:
- relaid_output: bfloat16 [2048, 4096], P('dp', 'tensor')
- input_grad: bfloat16 [2048, 4096], P('dp', 'tensor')
Inputs may be any that keep to these rules, and one draw needn't show every extreme that they name: `doc_lengths`: each row lists the lengths of the documents packed on that dp index in order: multiples of 128, the nonzero ones first, summing to 256. In every draw some dp index holds a single document of 256 tokens. `block_owner`: every dp index owns exactly one block of each position j < 8 and exactly one block from each dp index. `norm_gain`: positive gains.
All inputs are finite; a program needn't handle non-finite values.
Results may differ from a plain program's by a relative error of at most 0.015.
Values may be sent and summed in bfloat16 or wider, within the bound.
No kernel may reach another device: no remote copies, remote signals or barrier semaphores. Data moves between devices by JAX's collectives and lax.ppermute only.
A program may use at most 128 MiB of HBM per device.

v0:
```python
import math
import jax
import jax.numpy as jnp
from jax import lax
from jax.sharding import PartitionSpec as P

HEAD_SIZE = 128
ROPE_BASE = 500000.0
NORM_EPSILON = 1e-05


def doc_tables(lengths_row, token_row_count):
    ends = jnp.cumsum(lengths_row)
    token_index = jnp.arange(token_row_count, dtype=jnp.int32)
    passed = (token_index[:, None] >= ends[None, :]).astype(jnp.int32)
    doc_ids = jnp.sum(passed, axis=1)
    starts = jnp.max(jnp.where(passed > 0, ends[None, :], 0), axis=1)
    return (doc_ids, token_index - starts)


def rope_tables(positions, head_size):
    half_dim = head_size // 2
    steps = jnp.arange(half_dim, dtype=jnp.float32)
    inverse_freq = jnp.power(ROPE_BASE, -2.0 * steps / head_size)
    angles = positions.astype(jnp.float32)[:, None] * inverse_freq[None, :]
    return (jnp.cos(angles), jnp.sin(angles))


def rotate(vectors, cosine, sine_table):
    half_dim = vectors.shape[-1] // 2
    former = vectors[..., :half_dim]
    latter = vectors[..., half_dim:]
    cos_part = cosine[:, None, :]
    sin_part = sine_table[:, None, :]
    return jnp.concatenate(
        [former * cos_part - latter * sin_part, latter * cos_part + former * sin_part], axis=-1
    )


def unrotate(vectors, cosine, sine_table):
    half_dim = vectors.shape[-1] // 2
    former = vectors[..., :half_dim]
    latter = vectors[..., half_dim:]
    cos_part = cosine[:, None, :]
    sin_part = sine_table[:, None, :]
    return jnp.concatenate(
        [former * cos_part + latter * sin_part, latter * cos_part - former * sin_part], axis=-1
    )


def per_device(
    tokens,
    norm_gain,
    w_query,
    key_weight,
    value_weight,
    w_out,
    grad_output,
    doc_lengths,
    block_owner,
):
    token_row_count, width_part = tokens.shape
    full_width = norm_gain.shape[0]
    sources = lax.axis_size("dp")
    data_index = lax.axis_index("dp")
    tensor_index = lax.axis_index("tensor")
    query_width = w_query.shape[1]
    key_width = key_weight.shape[1]
    heads_local = query_width // HEAD_SIZE
    kv_local = key_width // HEAD_SIZE
    query_group_width = heads_local // kv_local
    scale_factor = 1.0 / math.sqrt(HEAD_SIZE)
    gain_part = lax.dynamic_slice_in_dim(norm_gain, tensor_index * width_part, width_part)
    w_joined = jnp.concatenate([w_query, key_weight, value_weight], axis=1)
    x_float = tokens.astype(jnp.float32)
    gathered = lax.all_gather(tokens, "tensor", axis=1, tiled=True)
    gathered_float = gathered.astype(jnp.float32)
    inverse = lax.rsqrt(jnp.mean(gathered_float * gathered_float, axis=1) + NORM_EPSILON)
    normed_input = (gathered_float * inverse[:, None] * norm_gain[None, :]).astype(jnp.bfloat16)
    projected = jnp.dot(normed_input, w_joined, preferred_element_type=jnp.float32)
    doc_ids, positions = doc_tables(doc_lengths[0], token_row_count)
    token_index = jnp.arange(token_row_count, dtype=jnp.int32)
    allowed = (doc_ids[:, None] == doc_ids[None, :]) & (
        token_index[None, :] <= token_index[:, None]
    )
    cosine, sine_table = rope_tables(positions, HEAD_SIZE)
    query_rows = rotate(
        projected[:, :query_width].reshape(token_row_count, heads_local, HEAD_SIZE),
        cosine,
        sine_table,
    ).astype(jnp.bfloat16)
    keys = rotate(
        projected[:, query_width : query_width + key_width].reshape(
            token_row_count, kv_local, HEAD_SIZE
        ),
        cosine,
        sine_table,
    ).astype(jnp.bfloat16)
    value_rows = (
        projected[:, query_width + key_width :]
        .astype(jnp.bfloat16)
        .reshape(token_row_count, kv_local, HEAD_SIZE)
    )
    grouped_query = query_rows.reshape(token_row_count, kv_local, query_group_width, HEAD_SIZE)
    scores = (
        jnp.einsum("qkgd,skd->kgqs", grouped_query, keys, preferred_element_type=jnp.float32)
        * scale_factor
    )
    weights = jnp.where(allowed[None, None], jnp.exp(scores), 0.0)
    probs = weights / jnp.sum(weights, axis=-1, keepdims=True)
    probs_low = probs.astype(jnp.bfloat16)
    attended = jnp.einsum(
        "kgqs,skd->qkgd", probs_low, value_rows, preferred_element_type=jnp.float32
    ).astype(jnp.bfloat16)
    attended_flat = attended.reshape(token_row_count, query_width)
    mixed_turned = lax.psum_scatter(
        lax.dot_general(
            w_out, attended_flat, (((0,), (1,)), ((), ())), preferred_element_type=jnp.float32
        ).astype(jnp.bfloat16),
        "tensor",
        scatter_dimension=0,
        tiled=True,
    ).astype(jnp.float32)
    output_home = (x_float + mixed_turned.T).astype(jnp.bfloat16)
    block_count = block_owner.shape[1]
    owner_row = lax.dynamic_slice_in_dim(block_owner, data_index, 1, 0)[0]
    slot_index = jnp.arange(sources, dtype=jnp.int32)
    send_table = (owner_row[None, :] == slot_index[:, None]).astype(jnp.bfloat16)
    owned_flags = jnp.sum((block_owner == data_index).astype(jnp.int32), axis=1)
    owned_rank = jnp.cumsum(owned_flags) - owned_flags
    block_index = jnp.arange(block_count, dtype=jnp.int32)
    keep_table = (
        (owned_rank[None, :] == block_index[:, None]) & (owned_flags[None, :] > 0)
    ).astype(jnp.bfloat16)
    home_blocks = output_home.reshape(block_count, -1)
    outgoing = jnp.dot(send_table, home_blocks, preferred_element_type=jnp.float32).astype(
        jnp.bfloat16
    )
    incoming = lax.all_to_all(outgoing, "dp", split_axis=0, concat_axis=0, tiled=True)
    relaid = (
        jnp.dot(keep_table, incoming, preferred_element_type=jnp.float32)
        .astype(jnp.bfloat16)
        .reshape(token_row_count, width_part)
    )
    owned_blocks = grad_output.reshape(block_count, -1)
    returning = lax.dot_general(
        keep_table, owned_blocks, (((0,), (0,)), ((), ())), preferred_element_type=jnp.float32
    ).astype(jnp.bfloat16)
    arrived = lax.all_to_all(returning, "dp", split_axis=0, concat_axis=0, tiled=True)
    grad_home = (
        lax.dot_general(
            send_table, arrived, (((0,), (0,)), ((), ())), preferred_element_type=jnp.float32
        )
        .astype(jnp.bfloat16)
        .reshape(token_row_count, width_part)
    )
    attended_gradient = lax.dot_general(
        lax.all_gather(grad_home, "tensor", axis=1, tiled=True),
        w_out,
        (((1,), (1,)), ((), ())),
        preferred_element_type=jnp.float32,
    ).astype(jnp.bfloat16)
    grouped_gradient = attended_gradient.reshape(
        token_row_count, kv_local, query_group_width, HEAD_SIZE
    )
    delta = jnp.sum(grouped_gradient.astype(jnp.float32) * attended.astype(jnp.float32), axis=-1)
    grad_probs = jnp.einsum(
        "qkgd,skd->kgqs", grouped_gradient, value_rows, preferred_element_type=jnp.float32
    )
    grad_scores = (probs * (grad_probs - jnp.transpose(delta, (1, 2, 0))[..., None])).astype(
        jnp.bfloat16
    )
    grad_query_rot = (
        jnp.einsum("kgqs,skd->qkgd", grad_scores, keys, preferred_element_type=jnp.float32)
        * scale_factor
    )
    grad_keys_rot = (
        jnp.einsum("kgqs,qkgd->skd", grad_scores, grouped_query, preferred_element_type=jnp.float32)
        * scale_factor
    )
    value_gradient = jnp.einsum(
        "kgqs,qkgd->skd", probs_low, grouped_gradient, preferred_element_type=jnp.float32
    )
    grad_query = unrotate(
        grad_query_rot.reshape(token_row_count, heads_local, HEAD_SIZE), cosine, sine_table
    ).astype(jnp.bfloat16)
    key_gradient = unrotate(grad_keys_rot, cosine, sine_table).astype(jnp.bfloat16)
    joined_grad = jnp.concatenate(
        [
            grad_query.reshape(token_row_count, query_width),
            key_gradient.reshape(token_row_count, key_width),
            value_gradient.astype(jnp.bfloat16).reshape(token_row_count, key_width),
        ],
        axis=1,
    )
    normed_gradient = (
        lax.psum_scatter(
            lax.dot_general(
                w_joined, joined_grad, (((1,), (1,)), ((), ())), preferred_element_type=jnp.float32
            ).astype(jnp.bfloat16),
            "tensor",
            scatter_dimension=0,
            tiled=True,
        )
        .astype(jnp.float32)
        .T
    )
    stat = (
        lax.psum(jnp.sum(normed_gradient * gain_part[None, :] * x_float, axis=1), "tensor")
        / full_width
    )
    cubed = inverse * inverse * inverse
    grad_x = (
        grad_home.astype(jnp.float32)
        + inverse[:, None] * gain_part[None, :] * normed_gradient
        - x_float * cubed[:, None] * stat[:, None]
    )
    return (relaid, grad_x.astype(jnp.bfloat16))


def solution(mesh):
    placed = (
        P("dp", "tensor"),
        P(),
        P(None, "tensor"),
        P(None, "tensor"),
        P(None, "tensor"),
        P("tensor", None),
        P("dp", "tensor"),
        P("dp", None),
        P(),
    )
    return jax.shard_map(
        per_device,
        mesh=mesh,
        in_specs=placed,
        out_specs=(P("dp", "tensor"), P("dp", "tensor")),
        check_vma=False,
    )
```

profile of v0, /device:TPU:0, one launch (start us, length us, event | category | flops | bytes accessed | tf_op | source)
XLA Modules:
  0.0 188.4 jit_solution(454758210394766941)
XLA Ops:
  7.2 0.7 all-gather.3.cloned.1.call-update
  7.9 1.3 reshape.232
  9.2 0.8 convert_reduce_fusion
  10.2 0.4 fusion.1
  10.6 0.6 broadcast.110
  11.1 1.1 reduce
  12.2 1.2 reshape.245
  13.4 7.3 %all-to-all-start.1 = ((bf16[8,2,16384]{2,1,0:T(2,128)(2,1)}), bf16[8,2,16384]{2,1,0:T(2,128)(2,1)S(1)}, u32[]{:S(2)}, u32[]{:S(2)}) async-start(bf16[8,2,16384]{2,1,0:T(2,128)(2,1)} %reshape.245), calls=%async_computation.2 | async-start | bytes 1048576 | tf_op jit(solution)/shard_map/all_to_all | solution.py:149
  20.9 0.7 dynamic-slice_bitcast_fusion
  21.8 7.9 %constant_dynamic-update-slice_fusion.2 = bf16[4096,1536]{1,0:T(8,128)(2,1)} fusion(bf16[4096,1024]{1,0:T(8,128)(2,1)} %param.11), kind=kLoop, calls=%fused_computation.78 | loop fusion | bytes 16777216
  29.7 1.6 constant_dynamic-update-slice_fusion.1
  31.3 0.8 copy-done.3
  32.1 1.7 constant_dynamic-update-slice_fusion
  33.8 1.4 all-to-all-done.1
  35.1 0.5 reshape.246
  35.7 0.7 convolution_convert_fusion
  36.4 1.0 reshape.233
  37.7 0.5 multiply_cosine_fusion
  38.2 2.2 %fusion.3 = f32[256]{0:T(256)S(1)} fusion(bf16[256,4096]{1,0:T(8,128)(2,1)} %all-gather.3.cloned.1.call-done), kind=kLoop, calls=%fused_computation.11 | loop fusion | flops 3145472 | bytes 2098176 | tf_op jit(solution)/shard_map/reduce_sum | solution.py:78
  40.5 6.8 %fusion.6 = f32[256,1536]{1,0:T(8,128)S(1)} fusion(bf16[4096,1536]{1,0:T(8,128)(2,1)} %constant_dynamic-update-slice_fusion, bf16[256,4096]{1,0:T(8,128)(2,1)S(1)} %copy-done.4, f32[4096]{0:T(1024)S(1)} %copy-done.11, f32[256]{0:T(256)S(1)} %get-tuple-element.21), kind=kOutput, calls=%fused_computation.14 | convolution fusion | flops 3225419776 | bytes 16270336 | tf_op jit(solution)/shard_map/dot_general | solution.py:80
  47.7 0.9 copy-done.5
  48.6 0.5 subtract_convert_fusion.1
  50.1 2.1 %fusion.13 = (f32[2,4,256]{2,1,0:T(4,128)S(1)}, f32[2,256,256,4]{2,1,3,0:T(8,128)}) fusion(pred[256,256]{0,1:T(8,128)(4,1)S(1)} %fusion.34, bf16[256,2,4,64]{3,0,2,1:T(8,128)(2,1)S(1)} %bitcast.116, bf16[256,2,4,64]{3,0,2,1:T(8,128)(2,1)S(1)} %bitcast.118, bf16[256,2,64]{2,0,1:T(8,128)(2,1)S(1)} %get-tuple-element.11, ...), kind=kOutput, calls=%fused_computation.22 | convolution fusion | flops 137099264 | bytes 2826240 | tf_op jit(solution)/shard_map/qkgd,skd->kgqs/dot_general | solution.py:106
  52.2 8.0 %all-gather.5.cloned.1.call-done = bf16[256,4096]{1,0:T(8,128)(2,1)} async-done(((bf16[256,1024]{1,0:T(8,128)(2,1)}), bf16[256,4096]{1,0:T(8,128)(2,1)}) %all-gather.5.cloned.1.call-update) | async-done | bytes 2097168 | tf_op jit(solution)/shard_map/all_gather | solution.py:158
  60.2 6.4 %convolution_convert_fusion.6 = bf16[256,1024]{1,0:T(8,128)(2,1)S(1)} fusion(bf16[256,4096]{1,0:T(8,128)(2,1)} %all-gather.5.cloned.1.call-done, bf16[1024,4096]{1,0:T(8,128)(2,1)} %param.14), kind=kOutput, calls=%fused_computation.27 | convolution fusion | flops 2147745792 | bytes 11010048 | tf_op jit(solution)/shard_map/dot_general | solution.py:157
  66.8 2.4 %fusion.16 = bf16[2,128,256]{2,1,0:T(8,128)(2,1)S(1)} fusion(bf16[256,2,4,128]{0,3,2,1:T(8,128)(2,1)S(1)} %bitcast.121, f32[2,256,256,4]{2,1,3,0:T(8,128)} %get-tuple-element.23, f32[2,4,256]{2,1,0:T(4,128)S(1)} %get-tuple-element.22, pred[256,256]{0,1:T(8,128)(4,1)S(1)} %fusion.34), kind=kOutput, calls=%fused_computation.33 | convolution fusion | flops 136380416 | bytes 2826240 | tf_op jit(solution)/shard_map/kgqs,qkgd->skd/dot_general | solution.py:181
  69.3 1.6 multiply_reduce_fusion
  70.8 0.7 fusion.9
  71.6 0.5 fusion.15
  72.1 0.4 convolution_multiply_fusion
  73.0 0.8 copy.117
  73.9 0.4 copy.145
  74.3 0.4 copy.144
  75.4 0.5 copy-done.6
  75.9 13.8 %convolution_convert_fusion.4 = bf16[4096,256]{0,1:T(8,128)(2,1)} fusion(bf16[4096,1536]{1,0:T(8,128)(2,1)} %constant_dynamic-update-slice_fusion, bf16[256,256]{1,0:T(8,128)(2,1)S(1)} %copy.118, bf16[256,256]{1,0:T(8,128)(2,1)S(1)} %copy-done.6, bf16[256,1024]{1,0:T(8,128)(2,1)S(1)} %bitcast.123), kind=kOutput, calls=%fused_computation.8 | convolution fusion | flops 3224633344 | bytes 15466496 | tf_op jit(solution)/shard_map/dot_general | solution.py:198
  89.8 7.1 %fusion.2 = bf16[4096,256]{0,1:T(8,128)(2,1)} fusion(bf16[256,1024]{0,1:T(8,128)(2,1)S(1)} %bitcast.120, bf16[1024,4096]{1,0:T(8,128)(2,1)} %param.14), kind=kOutput, calls=%fused_computation.10 | convolution fusion | flops 2148532224 | bytes 11010048 | tf_op jit(solution)/shard_map/dot_general | solution.py:117
  96.9 0.8 dynamic_slice.7
  97.7 23.6 %reduce-scatter.5.cloned.1.call-done = bf16[1024,256]{0,1:T(8,128)(2,1)} async-done(((bf16[4096,256]{0,1:T(8,128)(2,1)}), bf16[1024,256]{0,1:T(8,128)(2,1)}) %reduce-scatter.5.cloned.1.call-update) | async-done | bytes 524304 | tf_op jit(solution)/shard_map/reduce_scatter | solution.py:197
  121.3 1.3 fusion.21
  122.6 5.8 %psum.7 = f32[256]{0:T(256)S(1)} all-reduce(f32[256]{0:T(256)S(1)} %fusion.21), channel_id=1, replica_groups=mesh['dp'=8,'tensor'=4] {'tensor'}, use_global_device_ids=true, to_apply=%region_11.12 | all-reduce | flops 256 | bytes 2048 | tf_op jit(solution)/shard_map/psum | solution.py:209
  128.4 26.9 %reduce-scatter.3.cloned.1.call-done = bf16[1024,256]{0,1:T(8,128)(2,1)} async-done(((bf16[4096,256]{0,1:T(8,128)(2,1)}), bf16[1024,256]{0,1:T(8,128)(2,1)}) %reduce-scatter.3.cloned.1.call-update) | async-done | bytes 524304 | tf_op jit(solution)/shard_map/reduce_scatter | solution.py:116
  155.3 2.5 %fusion.20 = (bf16[256,1024]{1,0:T(8,128)(2,1)}, bf16[256,1024]{1,0:T(8,128)(2,1)S(1)}) fusion(bf16[256,1024]{1,0:T(8,128)(2,1)S(1)} %copy-done, bf16[1024,256]{0,1:T(8,128)(2,1)} %reduce-scatter.5.cloned.1.call-done, bf16[256,1024]{1,0:T(8,128)(2,1)S(1)} %copy-done.1, f32[256]{0:T(256)S(1)} %broadcast_multiply_fusion, f32[256]{0:T(256)S(1)} %get-tuple-element.20, ...), kind=kLoop, calls=%fused_computation.37 | loop fusion | flops 3407872 | bytes 3152896 | tf_op jit(solution)/shard_map/convert_element_type | solution.py:218
  158.3 1.1 reduce.1
  159.4 0.4 reshape.243
  159.8 19.9 %all_to_all.24 = bf16[8,2,16384]{2,1,0:T(2,128)(2,1)S(1)} all-to-all(bf16[8,2,16384]{2,1,0:T(2,128)(2,1)S(1)} %reshape.243), channel_id=1, replica_groups=mesh['dp'=8,'tensor'=4] {'dp'}, dimensions={0} | all-to-all | bytes 1048576 | tf_op jit(solution)/shard_map/all_to_all | solution.py:139
  179.6 0.5 reshape.244
  180.2 0.7 convolution_convert_fusion.2
  180.8 1.0 reshape.231
  (65 shorter events, 4.3 us)
Async XLA Ops:
  7.2 31.1 %all-gather.3.cloned.1.call-start = ((), (), s32[]{:S(2)}) async-start(), calls=%async_computation.4 | async-start | bytes 2621440 | tf_op jit(solution)/shard_map/all_gather | solution.py:76
  10.2 10.5 %copy-start.12 = (s32[1,2]{1,0:T(1,128)S(1)}, s32[1,2]{1,0:T(1,128)}, u32[]{:S(2)}) copy-start(s32[1,2]{1,0:T(1,128)} %param.16) | copy-start | bytes 28
  13.4 21.7 %all-to-all-start.1 = ((bf16[8,2,16384]{2,1,0:T(2,128)(2,1)}), bf16[8,2,16384]{2,1,0:T(2,128)(2,1)S(1)}, u32[]{:S(2)}, u32[]{:S(2)}) async-start(bf16[8,2,16384]{2,1,0:T(2,128)(2,1)} %reshape.245), calls=%async_computation.2 | async-start | bytes 1048576 | tf_op jit(solution)/shard_map/all_to_all | solution.py:149
  20.6 39.6 %all-gather.5.cloned.1.call-start = ((), (), s32[]{:S(2)}) async-start(), calls=%async_computation.6 | async-start | bytes 2621440 | tf_op jit(solution)/shard_map/all_gather | solution.py:158
  21.6 14.1 %copy-start.9 = (s32[8]{0:T(128)}, s32[8]{0:T(128)S(1)}, u32[]{:S(2)}) copy-start(s32[8]{0:T(128)S(1)} %dynamic-slice_bitcast_fusion) | copy-start | bytes 100
  21.8 45.1 %copy-start.7 = (pred[256,256]{0,1:T(8,128)(4,1)}, pred[256,256]{0,1:T(8,128)(4,1)S(1)}, u32[]{:S(2)}) copy-start(pred[256,256]{0,1:T(8,128)(4,1)S(1)} %fusion.34) | copy-start | bytes 196612
  21.8 7.9 %copy-start.2 = (bf16[4096,256]{1,0:T(8,128)(2,1)S(1)}, bf16[4096,256]{1,0:T(8,128)(2,1)}, u32[]{:S(2)}) copy-start(bf16[4096,256]{1,0:T(8,128)(2,1)} %param.12) | copy-start | bytes 6291460
  29.7 2.4 %copy-start.3 = (bf16[4096,256]{1,0:T(8,128)(2,1)S(1)}, bf16[4096,256]{1,0:T(8,128)(2,1)}, u32[]{:S(2)}) copy-start(bf16[4096,256]{1,0:T(8,128)(2,1)} %param.13) | copy-start | bytes 6291460
  36.4 4.1 %copy-start.11 = (f32[4096]{0:T(1024)S(1)}, f32[4096]{0:T(1024)}, u32[]{:S(2)}) copy-start(f32[4096]{0:T(1024)} %param.10) | copy-start | bytes 49156
  37.4 83.9 %reduce-scatter.5.cloned.1.call-start = ((), (), s32[]{:S(2)}) async-start(), calls=%async_computation.7 | async-start | bytes 2621440 | tf_op jit(solution)/shard_map/reduce_scatter | solution.py:197
  38.2 2.3 %copy-start.4 = (bf16[256,4096]{1,0:T(8,128)(2,1)S(1)}, bf16[256,4096]{1,0:T(8,128)(2,1)}, u32[]{:S(2)}) copy-start(bf16[256,4096]{1,0:T(8,128)(2,1)} %all-gather.3.cloned.1.call-done) | copy-start | bytes 6291460
  47.4 1.2 copy-start.5
  48.6 0.9 slice-start
  66.8 2.4 %copy-start.13 = (f32[2,256,256,4]{2,1,3,0:T(8,128)S(1)}, f32[2,256,256,4]{2,1,3,0:T(8,128)}, u32[]{:S(2)}) copy-start(f32[2,256,256,4]{2,1,3,0:T(8,128)} %get-tuple-element.23) | copy-start | bytes 6291460
  69.2 1.6 copy-start.8
  75.0 0.9 copy-start.6
  89.7 65.6 %reduce-scatter.3.cloned.1.call-start = ((), (), s32[]{:S(2)}) async-start(), calls=%async_computation.5 | async-start | bytes 2621440 | tf_op jit(solution)/shard_map/reduce_scatter | solution.py:116
  96.9 24.4 %copy-start = (bf16[256,1024]{1,0:T(8,128)(2,1)S(1)}, bf16[256,1024]{1,0:T(8,128)(2,1)}, u32[]{:S(2)}) copy-start(bf16[256,1024]{1,0:T(8,128)(2,1)} %param.9) | copy-start | bytes 1572868
  96.9 58.4 %copy-start.1 = (bf16[256,1024]{1,0:T(8,128)(2,1)S(1)}, bf16[256,1024]{1,0:T(8,128)(2,1)}, u32[]{:S(2)}) copy-start(bf16[256,1024]{1,0:T(8,128)(2,1)} %reshape.233) | copy-start | bytes 1572868
  155.3 2.7 %copy-start.10 = (s32[8]{0:T(128)S(1)}, s32[8]{0:T(128)}, u32[]{:S(2)}) copy-start(s32[8]{0:T(128)} %copy-done.9) | copy-start | bytes 100
Sparse Core Ops, SparseCore 0:
  9.6 25.2 all-gather.2
  37.5 22.6 all-gather.4
  89.9 31.4 reduce-scatter.4
  123.9 31.3 reduce-scatter.2
where the time goes:
time: 189 us; the launch traced here: 188 us
  waiting for transfers between devices  60.6 us (32%)
  matrix products  43.8 us (23%)
  blocking collectives  25.6 us (14%)
  local copies, waits for them, and re-layouts  25.1 us (13%)
  between operations  14.2 us (8%)
  other arithmetic  11.4 us (6%)
  starting transfers between devices  7.59 us (4%)
    reduce_scatter x1, waiting for transfers between devices, per_device(): lax.psum_scatter(lax.dot_general(w_out, attended_flat, (((0,), (1,)), (()...  26.9 us
    reduce_scatter x1, waiting for transfers between devices, per_device(): lax.psum_scatter(lax.dot_general(w_joined, joined_grad, (((1,), (1,)), ((...  23.6 us
    all_to_all x1, blocking collectives, per_device(): lax.all_to_all(outgoing, 'dp', split_axis=0, concat_axis=0, tiled=True)  19.9 us
    unnamed x39, local copies, waits for them, and re-layouts  15.5 us
    dot_general x1, matrix products, per_device(): lax.dot_general(w_joined, joined_grad, (((1,), (1,)), ((), ())), preferre...  13.8 us
    all_gather x1, waiting for transfers between devices, per_device(): lax.all_gather(grad_home, 'tensor', axis=1, tiled=True)  7.99 us
    all_to_all x1, starting transfers between devices, per_device(): lax.all_to_all(returning, 'dp', split_axis=0, concat_axis=0, tiled=True)  7.25 us
    dot_general x1, matrix products, per_device(): lax.dot_general(w_out, attended_flat, (((0,), (1,)), ((), ())), preferred...  7.11 us
  transfers between devices with their start and end apart: 5, of which 4 were waited for; matrix products, arithmetic and copies ran while one was open for 23% of the time, Pallas kernels for 0%

commit v1 on v0

--- a/solution.py
+++ b/solution.py
@@ -7,6 +7,11 @@
 HEAD_SIZE = 128
 ROPE_BASE = 500000.0
 NORM_EPSILON = 1e-05
+
+
+def add_all(shard, axis):
+    parts = lax.all_gather(shard, axis)
+    return jnp.sum(parts, axis=0)
 
 
 def doc_tables(lengths_row, token_row_count):
@@ -206,7 +211,7 @@
         .T
     )
     stat = (
-        lax.psum(jnp.sum(normed_gradient * gain_part[None, :] * x_float, axis=1), "tensor")
+        add_all(jnp.sum(normed_gradient * gain_part[None, :] * x_float, axis=1), "tensor")
         / full_width
     )
     cubed = inverse * inverse * inverse

time: 189 us -> 189 us (level)
    psum x1 -> x0, blocking collectives: 5.76 us -> none  [per_device(): lax.psum(jnp.sum(normed_gradient * gain_part[None, :] * x_float, axis=1),...]
    all_gather x0 -> x1, blocking collectives: none -> 5.07 us  [add_all(): parts = lax.all_gather(shard, axis)]
where the time goes in v1:
time: 189 us; the launch traced here: 188 us
  waiting for transfers between devices  61.3 us (32%)
  matrix products  43.8 us (23%)
  local copies, waits for them, and re-layouts  25.1 us (13%)
  blocking collectives  24.9 us (13%)
  between operations  14.2 us (8%)
  other arithmetic  11.5 us (6%)
  starting transfers between devices  7.59 us (4%)
    reduce_scatter x1, waiting for transfers between devices, per_device(): lax.psum_scatter(lax.dot_general(w_out, attended_flat, (((0,), (1,)), (()...  27.6 us
    reduce_scatter x1, waiting for transfers between devices, per_device(): lax.psum_scatter(lax.dot_general(w_joined, joined_grad, (((1,), (1,)), ((...  23.6 us
    all_to_all x1, blocking collectives, per_device(): lax.all_to_all(outgoing, 'dp', split_axis=0, concat_axis=0, tiled=True)  19.9 us
    unnamed x39, local copies, waits for them, and re-layouts  15.5 us
    dot_general x1, matrix products, per_device(): lax.dot_general(w_joined, joined_grad, (((1,), (1,)), ((), ())), preferre...  13.8 us
    all_gather x1, waiting for transfers between devices, per_device(): lax.all_gather(grad_home, 'tensor', axis=1, tiled=True)  7.99 us
    all_to_all x1, starting transfers between devices, per_device(): lax.all_to_all(returning, 'dp', split_axis=0, concat_axis=0, tiled=True)  7.25 us
    dot_general x1, matrix products, per_device(): lax.dot_general(w_out, attended_flat, (((0,), (1,)), ((), ())), preferred...  7.11 us
  transfers between devices with their start and end apart: 5, of which 4 were waited for; matrix products, arithmetic and copies ran while one was open for 23% of the time, Pallas kernels for 0%

profile of v1, /device:TPU:0, one launch (start us, length us, event | category | flops | bytes accessed | tf_op | source)
XLA Modules:
  0.0 188.4 jit_solution(12962008922975050886)
XLA Ops:
  7.2 0.7 all-gather.5.cloned.1.call-update
  7.9 1.3 reshape.234
  9.2 0.8 convert_reduce_fusion
  10.2 0.4 fusion.1
  10.6 0.6 broadcast.113
  11.1 1.1 reduce.1
  12.2 1.2 reshape.251
  13.4 7.3 %all-to-all-start.1 = ((bf16[8,2,16384]{2,1,0:T(2,128)(2,1)}), bf16[8,2,16384]{2,1,0:T(2,128)(2,1)S(1)}, u32[]{:S(2)}, u32[]{:S(2)}) async-start(bf16[8,2,16384]{2,1,0:T(2,128)(2,1)} %reshape.251), calls=%async_computation.2 | async-start | bytes 1048576 | tf_op jit(solution)/shard_map/all_to_all | solution.py:154
  20.9 0.7 dynamic-slice_bitcast_fusion
  21.8 7.9 %constant_dynamic-update-slice_fusion.2 = bf16[4096,1536]{1,0:T(8,128)(2,1)} fusion(bf16[4096,1024]{1,0:T(8,128)(2,1)} %param.11), kind=kLoop, calls=%fused_computation.78 | loop fusion | bytes 16777216
  29.7 1.6 constant_dynamic-update-slice_fusion.1
  31.3 0.8 copy-done.3
  32.1 1.7 constant_dynamic-update-slice_fusion
  33.8 1.4 all-to-all-done.1
  35.1 0.5 reshape.252
  35.7 0.7 convolution_convert_fusion
  36.4 1.0 reshape.235
  37.7 0.5 multiply_cosine_fusion
  38.2 2.2 %fusion.3 = f32[256]{0:T(256)S(1)} fusion(bf16[256,4096]{1,0:T(8,128)(2,1)} %all-gather.5.cloned.1.call-done), kind=kLoop, calls=%fused_computation.11 | loop fusion | flops 3145472 | bytes 2098176 | tf_op jit(solution)/shard_map/reduce_sum | solution.py:83
  40.5 6.8 %fusion.6 = f32[256,1536]{1,0:T(8,128)S(1)} fusion(bf16[4096,1536]{1,0:T(8,128)(2,1)} %constant_dynamic-update-slice_fusion, bf16[256,4096]{1,0:T(8,128)(2,1)S(1)} %copy-done.4, f32[4096]{0:T(1024)S(1)} %copy-done.11, f32[256]{0:T(256)S(1)} %get-tuple-element.21), kind=kOutput, calls=%fused_computation.14 | convolution fusion | flops 3225419776 | bytes 16270336 | tf_op jit(solution)/shard_map/dot_general | solution.py:85
  47.7 0.9 copy-done.5
  48.6 0.5 subtract_convert_fusion.1
  50.1 2.1 %fusion.13 = (f32[2,4,256]{2,1,0:T(4,128)S(1)}, f32[2,256,256,4]{2,1,3,0:T(8,128)}) fusion(pred[256,256]{0,1:T(8,128)(4,1)S(1)} %fusion.34, bf16[256,2,4,64]{3,0,2,1:T(8,128)(2,1)S(1)} %bitcast.117, bf16[256,2,4,64]{3,0,2,1:T(8,128)(2,1)S(1)} %bitcast.119, bf16[256,2,64]{2,0,1:T(8,128)(2,1)S(1)} %get-tuple-element.11, ...), kind=kOutput, calls=%fused_computation.22 | convolution fusion | flops 137099264 | bytes 2826240 | tf_op jit(solution)/shard_map/qkgd,skd->kgqs/dot_general | solution.py:111
  52.2 8.0 %all-gather.7.cloned.1.call-done = bf16[256,4096]{1,0:T(8,128)(2,1)} async-done(((bf16[256,1024]{1,0:T(8,128)(2,1)}), bf16[256,4096]{1,0:T(8,128)(2,1)}) %all-gather.7.cloned.1.call-update) | async-done | bytes 2097168 | tf_op jit(solution)/shard_map/all_gather | solution.py:163
  60.2 6.4 %convolution_convert_fusion.6 = bf16[256,1024]{1,0:T(8,128)(2,1)S(1)} fusion(bf16[256,4096]{1,0:T(8,128)(2,1)} %all-gather.7.cloned.1.call-done, bf16[1024,4096]{1,0:T(8,128)(2,1)} %param.14), kind=kOutput, calls=%fused_computation.27 | convolution fusion | flops 2147745792 | bytes 11010048 | tf_op jit(solution)/shard_map/dot_general | solution.py:162
  66.8 2.4 %fusion.16 = bf16[2,128,256]{2,1,0:T(8,128)(2,1)S(1)} fusion(bf16[256,2,4,128]{0,3,2,1:T(8,128)(2,1)S(1)} %bitcast.122, f32[2,256,256,4]{2,1,3,0:T(8,128)} %get-tuple-element.23, f32[2,4,256]{2,1,0:T(4,128)S(1)} %get-tuple-element.22, pred[256,256]{0,1:T(8,128)(4,1)S(1)} %fusion.34), kind=kOutput, calls=%fused_computation.33 | convolution fusion | flops 136380416 | bytes 2826240 | tf_op jit(solution)/shard_map/kgqs,qkgd->skd/dot_general | solution.py:186
  69.3 1.6 multiply_reduce_fusion
  70.8 0.7 fusion.9
  71.6 0.5 fusion.15
  72.1 0.4 convolution_multiply_fusion
  73.0 0.8 copy.117
  73.9 0.4 copy.145
  74.3 0.4 copy.144
  75.4 0.5 copy-done.6
  75.9 13.8 %convolution_convert_fusion.4 = bf16[4096,256]{0,1:T(8,128)(2,1)} fusion(bf16[4096,1536]{1,0:T(8,128)(2,1)} %constant_dynamic-update-slice_fusion, bf16[256,256]{1,0:T(8,128)(2,1)S(1)} %copy.118, bf16[256,256]{1,0:T(8,128)(2,1)S(1)} %copy-done.6, bf16[256,1024]{1,0:T(8,128)(2,1)S(1)} %bitcast.124), kind=kOutput, calls=%fused_computation.8 | convolution fusion | flops 3224633344 | bytes 15466496 | tf_op jit(solution)/shard_map/dot_general | solution.py:203
  89.8 7.1 %fusion.2 = bf16[4096,256]{0,1:T(8,128)(2,1)} fusion(bf16[256,1024]{0,1:T(8,128)(2,1)S(1)} %bitcast.121, bf16[1024,4096]{1,0:T(8,128)(2,1)} %param.14), kind=kOutput, calls=%fused_computation.10 | convolution fusion | flops 2148532224 | bytes 11010048 | tf_op jit(solution)/shard_map/dot_general | solution.py:122
  96.9 0.8 dynamic_slice.7
  97.7 23.6 %reduce-scatter.5.cloned.1.call-done = bf16[1024,256]{0,1:T(8,128)(2,1)} async-done(((bf16[4096,256]{0,1:T(8,128)(2,1)}), bf16[1024,256]{0,1:T(8,128)(2,1)}) %reduce-scatter.5.cloned.1.call-update) | async-done | bytes 524304 | tf_op jit(solution)/shard_map/reduce_scatter | solution.py:202
  121.3 1.3 fusion.21
  122.6 5.1 %all-gather.1 = f32[4,1,256]{2,1,0:T(1,128)S(1)} all-gather(f32[1,1,256]{2,1,0:T(1,128)S(1)} %bitcast.129), channel_id=2, replica_groups=mesh['dp'=8,'tensor'=4] {'tensor'}, dimensions={0}, use_global_device_ids=true | all-gather | bytes 5120 | tf_op jit(solution)/shard_map/all_gather | solution.py:13
  127.7 27.6 %reduce-scatter.3.cloned.1.call-done = bf16[1024,256]{0,1:T(8,128)(2,1)} async-done(((bf16[4096,256]{0,1:T(8,128)(2,1)}), bf16[1024,256]{0,1:T(8,128)(2,1)}) %reduce-scatter.3.cloned.1.call-update) | async-done | bytes 524304 | tf_op jit(solution)/shard_map/reduce_scatter | solution.py:121
  155.3 2.5 %fusion.20 = (bf16[256,1024]{1,0:T(8,128)(2,1)}, bf16[256,1024]{1,0:T(8,128)(2,1)S(1)}) fusion(bf16[256,1024]{1,0:T(8,128)(2,1)S(1)} %copy-done, bf16[1024,256]{0,1:T(8,128)(2,1)} %reduce-scatter.5.cloned.1.call-done, bf16[256,1024]{1,0:T(8,128)(2,1)S(1)} %copy-done.1, f32[256]{0:T(256)S(1)} %broadcast_multiply_fusion, f32[256]{0:T(256)S(1)} %get-tuple-element.20, ...), kind=kLoop, calls=%fused_computation.37 | loop fusion | flops 3407872 | bytes 3152896 | tf_op jit(solution)/shard_map/convert_element_type | solution.py:223
  158.3 1.1 reduce.2
  159.4 0.4 reshape.249
  159.8 19.9 %all_to_all.24 = bf16[8,2,16384]{2,1,0:T(2,128)(2,1)S(1)} all-to-all(bf16[8,2,16384]{2,1,0:T(2,128)(2,1)S(1)} %reshape.249), channel_id=1, replica_groups=mesh['dp'=8,'tensor'=4] {'dp'}, dimensions={0} | all-to-all | bytes 1048576 | tf_op jit(solution)/shard_map/all_to_all | solution.py:144
  179.6 0.5 reshape.250
  180.2 0.7 convolution_convert_fusion.2
  180.8 1.0 reshape.233
  (66 shorter events, 4.4 us)
Async XLA Ops:
  7.2 31.1 %all-gather.5.cloned.1.call-start = ((), (), s32[]{:S(2)}) async-start(), calls=%async_computation.4 | async-start | bytes 2621440 | tf_op jit(solution)/shard_map/all_gather | solution.py:81
  10.2 10.5 %copy-start.12 = (s32[1,2]{1,0:T(1,128)S(1)}, s32[1,2]{1,0:T(1,128)}, u32[]{:S(2)}) copy-start(s32[1,2]{1,0:T(1,128)} %param.16) | copy-start | bytes 28
  13.4 21.7 %all-to-all-start.1 = ((bf16[8,2,16384]{2,1,0:T(2,128)(2,1)}), bf16[8,2,16384]{2,1,0:T(2,128)(2,1)S(1)}, u32[]{:S(2)}, u32[]{:S(2)}) async-start(bf16[8,2,16384]{2,1,0:T(2,128)(2,1)} %reshape.251), calls=%async_computation.2 | async-start | bytes 1048576 | tf_op jit(solution)/shard_map/all_to_all | solution.py:154
  20.6 39.6 %all-gather.7.cloned.1.call-start = ((), (), s32[]{:S(2)}) async-start(), calls=%async_computation.6 | async-start | bytes 2621440 | tf_op jit(solution)/shard_map/all_gather | solution.py:163
  21.6 14.1 %copy-start.9 = (s32[8]{0:T(128)}, s32[8]{0:T(128)S(1)}, u32[]{:S(2)}) copy-start(s32[8]{0:T(128)S(1)} %dynamic-slice_bitcast_fusion) | copy-start | bytes 100
  21.8 45.1 %copy-start.7 = (pred[256,256]{0,1:T(8,128)(4,1)}, pred[256,256]{0,1:T(8,128)(4,1)S(1)}, u32[]{:S(2)}) copy-start(pred[256,256]{0,1:T(8,128)(4,1)S(1)} %fusion.34) | copy-start | bytes 196612
  21.8 7.9 %copy-start.2 = (bf16[4096,256]{1,0:T(8,128)(2,1)S(1)}, bf16[4096,256]{1,0:T(8,128)(2,1)}, u32[]{:S(2)}) copy-start(bf16[4096,256]{1,0:T(8,128)(2,1)} %param.12) | copy-start | bytes 6291460
  29.7 2.4 %copy-start.3 = (bf16[4096,256]{1,0:T(8,128)(2,1)S(1)}, bf16[4096,256]{1,0:T(8,128)(2,1)}, u32[]{:S(2)}) copy-start(bf16[4096,256]{1,0:T(8,128)(2,1)} %param.13) | copy-start | bytes 6291460
  36.4 4.1 %copy-start.11 = (f32[4096]{0:T(1024)S(1)}, f32[4096]{0:T(1024)}, u32[]{:S(2)}) copy-start(f32[4096]{0:T(1024)} %param.10) | copy-start | bytes 49156
  37.4 83.9 %reduce-scatter.5.cloned.1.call-start = ((), (), s32[]{:S(2)}) async-start(), calls=%async_computation.7 | async-start | bytes 2621440 | tf_op jit(solution)/shard_map/reduce_scatter | solution.py:202
  38.2 2.3 %copy-start.4 = (bf16[256,4096]{1,0:T(8,128)(2,1)S(1)}, bf16[256,4096]{1,0:T(8,128)(2,1)}, u32[]{:S(2)}) copy-start(bf16[256,4096]{1,0:T(8,128)(2,1)} %all-gather.5.cloned.1.call-done) | copy-start | bytes 6291460
  47.4 1.2 copy-start.5
  48.6 0.9 slice-start
  66.8 2.4 %copy-start.13 = (f32[2,256,256,4]{2,1,3,0:T(8,128)S(1)}, f32[2,256,256,4]{2,1,3,0:T(8,128)}, u32[]{:S(2)}) copy-start(f32[2,256,256,4]{2,1,3,0:T(8,128)} %get-tuple-element.23) | copy-start | bytes 6291460
  69.2 1.6 copy-start.8
  75.0 0.9 copy-start.6
  89.7 65.6 %reduce-scatter.3.cloned.1.call-start = ((), (), s32[]{:S(2)}) async-start(), calls=%async_computation.5 | async-start | bytes 2621440 | tf_op jit(solution)/shard_map/reduce_scatter | solution.py:121
  96.9 24.4 %copy-start = (bf16[256,1024]{1,0:T(8,128)(2,1)S(1)}, bf16[256,1024]{1,0:T(8,128)(2,1)}, u32[]{:S(2)}) copy-start(bf16[256,1024]{1,0:T(8,128)(2,1)} %param.9) | copy-start | bytes 1572868
  96.9 58.4 %copy-start.1 = (bf16[256,1024]{1,0:T(8,128)(2,1)S(1)}, bf16[256,1024]{1,0:T(8,128)(2,1)}, u32[]{:S(2)}) copy-start(bf16[256,1024]{1,0:T(8,128)(2,1)} %reshape.235) | copy-start | bytes 1572868
  155.3 2.7 %copy-start.10 = (s32[8]{0:T(128)S(1)}, s32[8]{0:T(128)}, u32[]{:S(2)}) copy-start(s32[8]{0:T(128)} %copy-done.9) | copy-start | bytes 100
Sparse Core Ops, SparseCore 0:
  9.6 25.2 all-gather.4
  37.5 22.6 all-gather.6
  89.9 31.4 reduce-scatter.4
  123.9 31.3 reduce-scatter.2
